TPU v7x, 32 devices: a whole 2x2x4 slice. The times are simulated.
32 devices in a mesh: seq: 16 (over z, y, x), tp: 2 (over core).
Axes of the slice: x: 2, y: 2, z: 4, core: 2. Of those that a mesh axis runs over, the one named last changes fastest.
Arguments:
- prefill_hidden: bfloat16 [2048, 5120], P('seq', 'tp'), may hold values from -14 to 14
- prefill_query_rows: bfloat16 [2048, 5120], P('seq', 'tp'), may hold values from -250 to 250
- prefill_key_value: bfloat16 [2, 2048, 1024], P(None, 'seq', 'tp'), may hold values from -5 to 5
- request_prefix_cache: bfloat16 [2, 16, 768, 1024], P(None, 'seq', None, 'tp'), may hold values from -5 to 5
- prefix_lengths: int32 [16], replicated, may hold values from 0 to 768, as said below
- decode_hidden: bfloat16 [4, 5120], P(None, 'tp'), may hold values from -14 to 14
- decode_query_rows: bfloat16 [4, 5120], P(None, 'tp'), may hold values from -250 to 250
- decode_kv: bfloat16 [2, 4, 1024], P(None, None, 'tp'), may hold values from -5 to 5
- decode_slot_cache: bfloat16 [2, 5, 2048, 1024], P(None, None, 'seq', 'tp'), may hold values from -5 to 5
- cache_lengths: int32 [4], replicated, may hold values from 512 to 2048, as said below
- slot_table: int32 [4], replicated, may hold values from 0 to 4, as said below
- out_weight: bfloat16 [5120, 5120], P('tp', 'seq'), may hold values from -0.078125 to 0.078125
- final_gain: bfloat16 [5120], replicated, may hold values from 0.5 to 1.5
- head_weight: bfloat16 [5120, 152064], P(None, ('seq', 'tp')), may hold values from -4 to 4
Outputs:
- prefill_out: bfloat16 [2048, 5120], P('seq', 'tp')
- decode_out: bfloat16 [4, 5120], P(None, 'tp')
- log_probs: float32 [20, 152064], P(None, ('seq', 'tp'))
Inputs may be any that keep to these rules, and one draw needn't show every extreme that they name: `prefix_lengths`: some request has no cached prefix and some has exactly 768 cached tokens. `cache_lengths`: some request has exactly 2048 cached tokens. `slot_table`: distinct slots.
All inputs are finite; a program needn't handle non-finite values.
Results may differ from a plain program's by a relative error of at most 0.0035.
Values may be sent and summed in bfloat16 or wider, within the bound.
No kernel may reach another device: no remote copies, remote signals or barrier semaphores. Data moves between devices by JAX's collectives and lax.ppermute only.
A program may use at most 128 MiB of HBM per device.

v0:
```python
import math
import jax
import jax.numpy as jnp
from jax import lax
from jax.sharding import PartitionSpec as P

QUERY_HEADS = 40
KEY_HEADS = 8
HEAD_SIZE = 128
neg_large = -1e30
exact = lax.Precision.HIGHEST
norm_eps = 1e-06


def merged(value, axis, join):
    pieces = jax.tree.map(lambda part: lax.all_gather(part, axis), value)
    head = jax.tree.map(lambda part: part[0], pieces)
    tail = jax.tree.map(lambda part: part[1:], pieces)
    subtotal, _ = lax.scan(lambda subtotal, piece: (join(subtotal, piece), None), head, tail)
    return subtotal


def join_parts(earlier, later):
    row_max = jnp.maximum(earlier[0], later[0])
    factor_one = jnp.exp(earlier[0] - row_max)
    factor_two = jnp.exp(later[0] - row_max)
    return (
        row_max,
        earlier[1] * factor_one + later[1] * factor_two,
        earlier[2] * factor_one[..., None] + later[2] * factor_two[..., None],
    )


def join_totals(earlier, later):
    row_max = jnp.maximum(earlier[0], later[0])
    return (
        row_max,
        earlier[1] * jnp.exp(earlier[0] - row_max) + later[1] * jnp.exp(later[0] - row_max),
    )


def local(
    prefill_hidden,
    prefill_query_rows,
    prefill_key_value,
    request_prefix_cache,
    prefix_lengths,
    decode_hidden,
    decode_query_rows,
    decode_kv,
    decode_slot_cache,
    cache_lengths,
    slot_table,
    out_weight,
    final_gain,
    head_weight,
):
    query_group_width = QUERY_HEADS // KEY_HEADS
    score_scale = 1.0 / math.sqrt(HEAD_SIZE)
    kv_local = prefill_key_value.shape[2] // HEAD_SIZE
    seq_index = lax.axis_index("seq")
    span_len = prefill_query_rows.shape[0]
    prefix_len = request_prefix_cache.shape[2]
    prefix_end = lax.dynamic_slice_in_dim(prefix_lengths, seq_index, 1)[0]
    query_matrix = prefill_query_rows.reshape(span_len, kv_local, query_group_width, HEAD_SIZE)
    joined_keys = jnp.concatenate([request_prefix_cache[0, 0], prefill_key_value[0]], 0).reshape(
        prefix_len + span_len, kv_local, HEAD_SIZE
    )
    value_matrix = jnp.concatenate([request_prefix_cache[1, 0], prefill_key_value[1]], 0).reshape(
        prefix_len + span_len, kv_local, HEAD_SIZE
    )
    key_place = jnp.arange(prefix_len + span_len)
    query_place = jnp.arange(span_len)
    live_mask = jnp.where(
        key_place[None, :] < prefix_len,
        key_place[None, :] < prefix_end,
        key_place[None, :] - prefix_len <= query_place[:, None],
    )
    scores = (
        jnp.einsum("rkgh,skh->kgrs", query_matrix, joined_keys, preferred_element_type=jnp.float32)
        * score_scale
    )
    masked = jnp.where(live_mask, scores, neg_large)
    row_max = jnp.max(masked, axis=-1, keepdims=True)
    weights = jnp.where(live_mask, jnp.exp(masked - row_max), 0.0)
    row_sum = jnp.sum(weights, axis=-1)
    weights_low = weights.astype(jnp.bfloat16)
    mixed = jnp.einsum(
        "kgrs,skh->rkgh", weights_low, value_matrix, preferred_element_type=jnp.float32
    )
    prefill_attention = (
        (mixed / jnp.transpose(row_sum, (2, 0, 1))[..., None])
        .astype(jnp.bfloat16)
        .reshape(span_len, -1)
    )
    decode_count = decode_query_rows.shape[0]
    ctx_local = decode_slot_cache.shape[2]
    chosen = jnp.take(decode_slot_cache, slot_table, axis=1)
    positions = seq_index * ctx_local + jnp.arange(ctx_local)
    decode_live = (positions[None, :] < cache_lengths[:, None])[:, None, None, :]
    decode_token_rows = decode_query_rows.reshape(
        decode_count, kv_local, query_group_width, HEAD_SIZE
    )
    cache_keys = chosen[0].reshape(decode_count, ctx_local, kv_local, HEAD_SIZE)
    cache_values = chosen[1].reshape(decode_count, ctx_local, kv_local, HEAD_SIZE)
    decode_scores = (
        jnp.einsum(
            "bkgh,bskh->bkgs", decode_token_rows, cache_keys, preferred_element_type=jnp.float32
        )
        * score_scale
    )
    decode_masked = jnp.where(decode_live, decode_scores, neg_large)
    decode_max = jnp.max(decode_masked, axis=-1)
    decode_weights = jnp.where(decode_live, jnp.exp(decode_masked - decode_max[..., None]), 0.0)
    decode_sum = jnp.sum(decode_weights, axis=-1)
    decode_mixed = jnp.einsum(
        "bkgs,bskh->bkgh", decode_weights, cache_values.astype(jnp.float32), precision=exact
    )
    best = lax.pmax(decode_max, "seq")
    factors = jnp.exp(decode_max - best)
    totals, mixtures = lax.psum((decode_sum * factors, decode_mixed * factors[..., None]), "seq")
    combined = (best, totals, mixtures)
    own_keys = decode_kv[0].reshape(decode_count, kv_local, HEAD_SIZE)
    own_values = decode_kv[1].reshape(decode_count, kv_local, HEAD_SIZE).astype(jnp.float32)
    own_scores = (
        jnp.einsum("bkgh,bkh->bkg", decode_token_rows, own_keys, preferred_element_type=jnp.float32)
        * score_scale
    )
    own_mixed = jnp.broadcast_to(own_values[:, :, None, :], combined[2].shape)
    final_max, final_sum, final_mixed = join_parts(
        combined, (own_scores, jnp.ones_like(own_scores), own_mixed)
    )
    decode_attention = (
        (final_mixed / final_sum[..., None]).astype(jnp.bfloat16).reshape(decode_count, -1)
    )
    attention_all = jnp.concatenate([prefill_attention, decode_attention], 0)
    every_row = lax.all_gather(attention_all, "seq", axis=0, tiled=True)
    column_block = jnp.dot(every_row, out_weight, preferred_element_type=jnp.float32)
    partial_terms = lax.all_to_all(column_block, "seq", split_axis=0, concat_axis=1, tiled=True)
    summed = lax.psum_scatter(partial_terms, "tp", scatter_dimension=1, tiled=True)
    residual = jnp.concatenate([prefill_hidden, decode_hidden], 0).astype(jnp.float32)
    updated = (residual + summed).astype(jnp.bfloat16)
    prefill_out = updated[:span_len]
    decode_out = updated[span_len:]
    gathered = lax.all_gather(prefill_out[span_len - 1 :], ("seq", "tp"), axis=0, tiled=True)
    decode_full = lax.all_gather(decode_out, "tp", axis=1, tiled=True)
    n_seq = lax.axis_size("seq")
    n_tp = lax.axis_size("tp")
    feature_width = prefill_out.shape[1]
    prefill_full = gathered.reshape(n_seq, n_tp * feature_width)
    head_input = jnp.concatenate([decode_full, prefill_full], 0).astype(jnp.float32)
    mean_square = jnp.mean(head_input * head_input, axis=-1, keepdims=True)
    normed = (
        head_input * lax.rsqrt(mean_square + norm_eps) * final_gain.astype(jnp.float32)
    ).astype(jnp.bfloat16)
    logits = jnp.dot(normed, head_weight, preferred_element_type=jnp.float32)
    local_max = jnp.max(logits, axis=-1)
    local_sum = jnp.sum(jnp.exp(logits - local_max[:, None]), axis=-1)
    global_max, global_sum = merged((local_max, local_sum), ("seq", "tp"), join_totals)
    log_probs = logits - (global_max + jnp.log(global_sum))[:, None]
    return (prefill_out, decode_out, log_probs)


def solution(mesh):
    return jax.shard_map(
        local,
        mesh=mesh,
        in_specs=(
            P("seq", "tp"),
            P("seq", "tp"),
            P(None, "seq", "tp"),
            P(None, "seq", None, "tp"),
            P(),
            P(None, "tp"),
            P(None, "tp"),
            P(None, None, "tp"),
            P(None, None, "seq", "tp"),
            P(),
            P(),
            P("tp", "seq"),
            P(),
            P(None, ("seq", "tp")),
        ),
        out_specs=(P("seq", "tp"), P(None, "tp"), P(None, ("seq", "tp"))),
        check_vma=False,
    )
```

profile of v0, /device:TPU:10, one launch (start us, length us, event | category | flops | bytes accessed | tf_op | source)
XLA Modules:
  0.0 531.2 jit_solution(17046051987952885032)
XLA Ops:
  8.7 1.9 gather_fusion
  11.7 31.6 %pmax.7 = f32[4,4,5]{2,1,0:T(4,128)S(1)} all-reduce(f32[4,4,5]{2,1,0:T(4,128)S(1)} %get-tuple-element.62), channel_id=1, replica_groups=mesh['seq'=16,'tp'=2] {'seq'}, use_global_device_ids=true, to_apply=%region_3.4 | all-reduce | flops 80 | bytes 640 | tf_op jit(solution)/shard_map/pmax | solution.py:119
  43.9 1.0 convolution_multiply_fusion.1
  44.9 74.1 %all-reduce.3 = (f32[4,4,5,128]{3,2,1,0:T(8,128)S(1)}, f32[4,4,5]{2,1,0:T(4,128)S(1)}) all-reduce(f32[4,4,5,128]{3,2,1,0:T(8,128)S(1)} %convolution_multiply_fusion.1, f32[4,4,5]{2,1,0:T(4,128)S(1)} %bitcast.100), channel_id=1, replica_groups=mesh['seq'=16,'tp'=2] {'seq'}, use_global_device_ids=true, to_apply=%region_4.5 | all-reduce | flops 10320 | bytes 82560 | tf_op jit(solution)/shard_map/psum | solution.py:121
  120.4 2.4 fusion.55
  122.7 1.4 copy.77
  124.1 1.2 copy.56
  125.3 1.7 fusion.57
  127.0 1.0 copy.78
  128.8 2.2 copy.58
  131.0 1.2 copy.52
  132.9 1.4 fusion.31
  134.3 7.4 %fusion.59 = (f32[4,5,128]{2,1,0:T(8,128)S(1)}, bf16[4,5,128,896]{2,3,1,0:T(8,128)(2,1)}) fusion(pred[128,896]{0,1:T(8,128)(4,1)} %fusion.31, bf16[128,4,5,128]{0,3,2,1:T(8,128)(2,1)} %bitcast.92, bf16[128,4,128]{2,0,1:T(8,128)(2,1)S(1)} %copy-done.5, bf16[768,4,128]{2,0,1:T(8,128)(2,1)S(1)} %copy-done.2), kind=kOutput, calls=%fused_computation.82 | convolution fusion | flops 602801024 | bytes 6285312 | tf_op jit(solution)/shard_map/sub | solution.py:85
  141.8 4.1 fusion.18
  145.9 1.3 copy.65
  147.2 0.9 maximum_bitcast_fusion.3
  148.4 143.1 %all-gather.6.cloned.1.call-done = bf16[16,132,2560]{2,1,0:T(8,128)(2,1)} async-done(((bf16[1,132,2560]{2,1,0:T(8,128)(2,1)}), bf16[16,132,2560]{2,1,0:T(8,128)(2,1)}) %all-gather.6.cloned.1.call-update) | async-done | bytes 10813456 | tf_op jit(solution)/shard_map/all_gather | solution.py:137
  291.5 11.0 %reshape.134 = bf16[2112,2560]{1,0:T(8,128)(2,1)} reshape(bf16[16,132,2560]{2,1,0:T(8,128)(2,1)} %all-gather.6.cloned.1.call-done) | data formatting | bytes 21626880
  302.5 10.3 %fusion.62 = f32[2112,320]{1,0:T(8,128)} fusion(bf16[2112,2560]{1,0:T(8,128)(2,1)} %reshape.134, bf16[2560,320]{0,1:T(8,128)(2,1)S(1)} %copy-done), kind=kOutput, calls=%fused_computation.85 | convolution fusion | flops 3460300800 | bytes 15155200 | tf_op jit(solution)/shard_map/dot_general | solution.py:138
  312.8 4.2 all_to_all.14
  317.0 80.1 %all_to_all.19 = f32[16,132,320]{2,1,0:T(8,128)S(1)} all-to-all(f32[16,132,320]{2,1,0:T(8,128)} %all_to_all.14), channel_id=1, replica_groups=mesh['seq'=16,'tp'=2] {'seq'}, dimensions={0} | all-to-all | bytes 5406720 | tf_op jit(solution)/shard_map/all_to_all | solution.py:139
  397.1 2.3 copy.67
  399.4 4.8 all_to_all.17
  404.2 10.2 %reduce-scatter.2.cloned.1.call-done = f32[132,2560]{1,0:T(8,128)} async-done(((f32[132,5120]{1,0:T(8,128)}), f32[132,2560]{1,0:T(8,128)}) %reduce-scatter.2.cloned.1.call-update) | async-done | bytes 1351696 | tf_op jit(solution)/shard_map/reduce_scatter | solution.py:140
  414.4 1.5 add_convert_fusion
  415.9 31.5 %all-gather.3 = bf16[32,1,2560]{2,1,0:T(2,128)(2,1)S(1)} all-gather(bf16[1,1,2560]{2,1,0:T(2,128)(2,1)S(1)} %slice_bitcast_fusion), channel_id=1, replica_groups=mesh['seq'=16,'tp'=2] {'seq','tp'}, dimensions={0}, use_global_device_ids=true | all-gather | bytes 168960 | tf_op jit(solution)/shard_map/all_gather | solution.py:145
  447.4 0.9 reduce
  448.4 1.8 all_gather.22
  450.5 19.8 %fusion.60 = (f32[20]{0:T(128)S(1)}, f32[20,4752]{1,0:T(8,128)S(1)}) fusion(bf16[5120,4752]{0,1:T(8,128)(2,1)} %param.29, f32[5120]{0:T(1024)S(1)} %convert_element_type.43, f32[20]{0:T(128)S(1)} %add_rsqrt_fusion, bf16[16,5120]{1,0:T(8,128)(2,1)S(1)} %reshape.110, bf16[4,5120]{1,0:T(4,128)(2,1)S(1)} %all_gather.22), kind=kOutput, calls=%fused_computation.83 | convolution fusion | flops 974021440 | bytes 49266080 | tf_op jit(solution)/shard_map/dot_general | solution.py:156
  471.0 49.9 %all-reduce.2 = (f32[640]{0:T(1024)S(1)}, f32[640]{0:T(1024)S(1)}) all-reduce(f32[640]{0:T(1024)S(1)} %dynamic-update-slice, f32[640]{0:T(1024)S(1)} %dynamic-update-slice.1), channel_id=2, replica_groups=mesh['seq'=16,'tp'=2] {'seq','tp'}, use_global_device_ids=true, to_apply=%add | all-reduce | flops 1280 | bytes 10240
  521.1 0.9 slice.69
  522.2 1.3 while.12
  (107 shorter events, 9.5 us)
Async XLA Ops:
  7.2 295.3 %copy-start = (bf16[2560,320]{0,1:T(8,128)(2,1)S(1)}, bf16[2560,320]{0,1:T(8,128)(2,1)}, u32[]{:S(2)}) copy-start(bf16[2560,320]{0,1:T(8,128)(2,1)} %param.27) | copy-start | bytes 4915204
  7.2 284.3 %all-gather.6.cloned.1.call-start = ((), (), s32[]{:S(2)}) async-start(), calls=%async_computation.3 | async-start | bytes 11837440 | tf_op jit(solution)/shard_map/all_gather | solution.py:137
  8.7 2.5 copy-start.9
  8.7 2.6 copy-start.12
  10.7 33.1 %copy-start.11 = (bf16[2,4,512]{2,1,0:T(4,128)(2,1)S(1)}, bf16[2,4,512]{2,1,0:T(4,128)(2,1)}, u32[]{:S(2)}) copy-start(bf16[2,4,512]{2,1,0:T(4,128)(2,1)} %param.23) | copy-start | bytes 24580
  10.8 108.3 %copy-start.13 = (s32[16]{0:T(128)S(1)}, s32[16]{0:T(128)}, u32[]{:S(2)}) copy-start(s32[16]{0:T(128)} %param.20) | copy-start | bytes 196
  125.3 9.0 %copy-start.2 = (bf16[768,4,128]{2,0,1:T(8,128)(2,1)S(1)}, bf16[768,4,128]{2,0,1:T(8,128)(2,1)}, u32[]{:S(2)}) copy-start(bf16[768,4,128]{2,0,1:T(8,128)(2,1)} %copy.56) | copy-start | bytes 2359300
  128.8 5.5 %copy-start.5 = (bf16[128,4,128]{2,0,1:T(8,128)(2,1)S(1)}, bf16[128,4,128]{2,0,1:T(8,128)(2,1)}, u32[]{:S(2)}) copy-start(bf16[128,4,128]{2,0,1:T(8,128)(2,1)} %copy.57) | copy-start | bytes 393220
  134.3 7.5 %copy-start.3 = (bf16[1,1,768,512]{2,3,1,0:T(8,128)(2,1)S(1)}, bf16[1,1,768,512]{2,3,1,0:T(8,128)(2,1)}, u32[]{:S(2)}) copy-start(bf16[1,1,768,512]{2,3,1,0:T(8,128)(2,1)} %copy.52) | copy-start | bytes 2359300
  134.3 7.5 %copy-start.6 = (bf16[1,128,512]{1,2,0:T(8,128)(2,1)S(1)}, bf16[1,128,512]{1,2,0:T(8,128)(2,1)}, u32[]{:S(2)}) copy-start(bf16[1,128,512]{1,2,0:T(8,128)(2,1)} %copy.53) | copy-start | bytes 393220
  148.2 266.2 %reduce-scatter.2.cloned.1.call-start = ((), (), s32[]{:S(2)}) async-start(), calls=%async_computation.2 | async-start | bytes 4177920 | tf_op jit(solution)/shard_map/reduce_scatter | solution.py:140
  399.4 4.8 copy-start.10
  399.4 15.0 %copy-start.4 = (bf16[128,2560]{1,0:T(8,128)(2,1)S(1)}, bf16[128,2560]{1,0:T(8,128)(2,1)}, u32[]{:S(2)}) copy-start(bf16[128,2560]{1,0:T(8,128)(2,1)} %param.16) | copy-start | bytes 1966084
  399.4 15.0 %copy-start.8 = (bf16[4,2560]{1,0:T(4,128)(2,1)S(1)}, bf16[4,2560]{1,0:T(4,128)(2,1)}, u32[]{:S(2)}) copy-start(bf16[4,2560]{1,0:T(4,128)(2,1)} %param.21) | copy-start | bytes 61444
  415.9 54.4 %copy-start.7 = (bf16[4,2560]{1,0:T(4,128)(2,1)}, bf16[4,2560]{1,0:T(4,128)(2,1)S(1)}, u32[]{:S(2)}) copy-start(bf16[4,2560]{1,0:T(4,128)(2,1)S(1)} %slice.70) | copy-start | bytes 61444
  450.5 73.9 %copy-start.1 = (bf16[2560,320]{0,1:T(8,128)(2,1)S(1)}, bf16[2560,320]{0,1:T(8,128)(2,1)}, u32[]{:S(2)}) copy-start(bf16[2560,320]{0,1:T(8,128)(2,1)} %param.27) | copy-start | bytes 4915204
Sparse Core Ops, SparseCore 0:
  148.3 143.1 all-gather.5
  404.3 10.0 reduce-scatter.1
where the time goes:
time: 532 us; the launch traced here: 531 us
  blocking collectives  269 us (51%)
  waiting for transfers between devices  153 us (29%)
  matrix products  43.1 us (8%)
  local copies, waits for them, and re-layouts  41.2 us (8%)
  between operations  14.4 us (3%)
  other arithmetic  9.66 us (2%)
    all_gather x1, waiting for transfers between devices, local(): every_row = lax.all_gather(attention_all, 'seq', axis=0, tiled=True)  143 us
    all_to_all x1, blocking collectives, local(): lax.all_to_all(column_block, 'seq', split_axis=0, concat_axis=1, tiled=True)  80.1 us
    psum x1, blocking collectives, local(): lax.psum((decode_sum * factors, decode_mixed * factors[..., None]), 'seq')  74.1 us
    unnamed x1, blocking collectives  49.9 us
    pmax x1, blocking collectives, local(): best = lax.pmax(decode_max, 'seq')  31.6 us
    all_gather x1, blocking collectives, local(): lax.all_gather(prefill_out[span_len - 1:], ('seq', 'tp'), axis=0, tiled=T...  31.5 us
    dot_general x1, matrix products, local(): logits = jnp.dot(normed, head_weight, preferred_element_type=jnp.float32)  19.8 us
    unnamed x37, local copies, waits for them, and re-layouts  16.2 us
  transfers between devices with their start and end apart: 2, of which 2 were waited for; matrix products, arithmetic and copies ran while one was open for 0% of the time, Pallas kernels for 0%

commit v1 on v0

--- a/solution.py
+++ b/solution.py
@@ -10,6 +10,37 @@
 neg_large = -1e30
 exact = lax.Precision.HIGHEST
 norm_eps = 1e-06
+
+
+def show_the_series_all(sheet, dim_no, body):
+    d_next, front = (sheet.shape[:dim_no], sheet.shape[dim_no + 1 :])
+    w1 = sheet.reshape(*d_next, body, -1, *front)
+    return jnp.moveaxis(w1, dim_no, 0)
+
+
+def block_name(xs, array_axis):
+    xs = jnp.moveaxis(xs, 0, array_axis)
+    latest = xs.shape
+    return xs.reshape(
+        *latest[:array_axis], latest[array_axis] * latest[array_axis + 1], *latest[array_axis + 2 :]
+    )
+
+
+def _draft_core(block_in, axis_name, z_in, shard_in):
+    u_next = lax.axis_size(axis_name)
+    low = lax.axis_index(axis_name)
+    v1, odd = (u_next, low)
+    even = show_the_series_all(block_in, z_in, v1)
+    nodes = [even[odd]]
+    for tick in [*range(1, v1)]:
+        w_next = even[odd ^ tick]
+        seen_now = lax.ppermute(
+            w_next, axis_name=axis_name, perm=[(ix, ix ^ tick) for ix in range(v1)]
+        )
+        nodes.append(seen_now)
+    z2 = jnp.stack(nodes, 0)
+    even = z2[odd ^ jnp.arange(v1)]
+    return block_name(even, shard_in)
 
 
 def merged(value, axis, join):
@@ -136,7 +167,7 @@
     attention_all = jnp.concatenate([prefill_attention, decode_attention], 0)
     every_row = lax.all_gather(attention_all, "seq", axis=0, tiled=True)
     column_block = jnp.dot(every_row, out_weight, preferred_element_type=jnp.float32)
-    partial_terms = lax.all_to_all(column_block, "seq", split_axis=0, concat_axis=1, tiled=True)
+    partial_terms = _draft_core(column_block, "seq", 0, 1)
     summed = lax.psum_scatter(partial_terms, "tp", scatter_dimension=1, tiled=True)
     residual = jnp.concatenate([prefill_hidden, decode_hidden], 0).astype(jnp.float32)
     updated = (residual + summed).astype(jnp.bfloat16)

time: 532 us -> 553 us (1.039)
  blocking collectives: 269 us -> 189 us
  waiting for transfers between devices: 153 us -> 205 us
  starting transfers between devices: 0.26 us -> 30.2 us
  local copies, waits for them, and re-layouts: 41.2 us -> 61.8 us
    all_to_all x1 -> x0, blocking collectives: 80.1 us -> none  [local(): lax.all_to_all(column_block, 'seq', split_axis=0, concat_axis=1, tiled=True)]
    ppermute x0 -> x15, waiting for transfers between devices: none -> 49.1 us  [_draft_core(): lax.ppermute(w_next, axis_name=axis_name, perm=[(ix, ix ^ tick) for ix in...]
    ppermute x0 -> x15, starting transfers between devices: none -> 29.9 us  [_draft_core(): lax.ppermute(w_next, axis_name=axis_name, perm=[(ix, ix ^ tick) for ix in...]
    all_to_all x3 -> x0, local copies, waits for them, and re-layouts: 11.2 us -> none  [local(): lax.all_to_all(column_block, 'seq', split_axis=0, concat_axis=1, tiled=True)]
    unnamed x37 -> x45, local copies, waits for them, and re-layouts: 16.2 us -> 26 us
    reshape x0 -> x2, local copies, waits for them, and re-layouts: none -> 8.97 us  [the longest x1 4.74 us: block_name(): xs.reshape(*latest[:array_axis], latest[array_axis] * latest[array_axis +...]
  transfers between devices with their start and end apart: 2 -> 17, of which waited for: 2 -> 13; matrix products, arithmetic and copies ran while one was open for 0% -> 2% of each run, Pallas kernels for 0% -> 0%
where the time goes in v1:
time: 553 us; the launch traced here: 552 us
  waiting for transfers between devices  205 us (37%)
  blocking collectives  189 us (34%)
  local copies, waits for them, and re-layouts  61.8 us (11%)
  matrix products  42.1 us (8%)
  starting transfers between devices  30.2 us (5%)
  between operations  14.5 us (3%)
  other arithmetic  9.08 us (2%)
    all_gather x1, waiting for transfers between devices, local(): every_row = lax.all_gather(attention_all, 'seq', axis=0, tiled=True)  143 us
    psum x1, blocking collectives, local(): lax.psum((decode_sum * factors, decode_mixed * factors[..., None]), 'seq')  74 us
    unnamed x1, blocking collectives  49.9 us
    ppermute x15, waiting for transfers between devices, _draft_core(): lax.ppermute(w_next, axis_name=axis_name, perm=[(ix, ix ^ tick) for ix in...  49.1 us
    pmax x1, blocking collectives, local(): best = lax.pmax(decode_max, 'seq')  31.6 us
    all_gather x1, blocking collectives, local(): lax.all_gather(prefill_out[span_len - 1:], ('seq', 'tp'), axis=0, tiled=T...  31.5 us
    ppermute x15, starting transfers between devices, _draft_core(): lax.ppermute(w_next, axis_name=axis_name, perm=[(ix, ix ^ tick) for ix in...  29.9 us
    unnamed x45, local copies, waits for them, and re-layouts  26 us
  transfers between devices with their start and end apart: 17, of which 13 were waited for; matrix products, arithmetic and copies ran while one was open for 2% of the time, Pallas kernels for 0%

profile of v1, /device:TPU:10, one launch (start us, length us, event | category | flops | bytes accessed | tf_op | source)
XLA Modules:
  0.0 551.6 jit_solution(16229846985475379854)
XLA Ops:
  10.6 2.4 fusion.56
  19.0 2.2 copy.58
  23.3 7.4 %fusion.60 = (f32[4,5,128]{2,1,0:T(8,128)S(1)}, bf16[4,5,128,896]{2,3,1,0:T(8,128)(2,1)}) fusion(pred[128,896]{0,1:T(8,128)(4,1)S(1)} %fusion.31, bf16[128,4,5,128]{0,3,2,1:T(8,128)(2,1)} %bitcast.154, bf16[128,4,128]{2,0,1:T(8,128)(2,1)} %copy.57, bf16[768,4,128]{2,0,1:T(8,128)(2,1)S(1)} %copy-done.2), kind=kOutput, calls=%fused_computation.117 | convolution fusion | flops 602801024 | bytes 6285312 | tf_op jit(solution)/shard_map/sub | solution.py:116
  30.7 3.3 fusion.18
  34.3 1.9 gather_fusion
  39.1 31.6 %pmax.7 = f32[4,4,5]{2,1,0:T(4,128)S(1)} all-reduce(f32[4,4,5]{2,1,0:T(4,128)S(1)} %get-tuple-element.78), channel_id=1, replica_groups=mesh['seq'=16,'tp'=2] {'seq'}, use_global_device_ids=true, to_apply=%region_3.4 | all-reduce | flops 80 | bytes 640 | tf_op jit(solution)/shard_map/pmax | solution.py:150
  72.3 74.0 %all-reduce.3 = (f32[4,4,5,128]{3,2,1,0:T(8,128)S(1)}, f32[4,4,5]{2,1,0:T(4,128)S(1)}) all-reduce(f32[4,4,5,128]{3,2,1,0:T(8,128)S(1)} %convolution_multiply_fusion.1, f32[4,4,5]{2,1,0:T(4,128)S(1)} %bitcast.162), channel_id=1, replica_groups=mesh['seq'=16,'tp'=2] {'seq'}, use_global_device_ids=true, to_apply=%region_4.5 | all-reduce | flops 10320 | bytes 82560 | tf_op jit(solution)/shard_map/psum | solution.py:152
  147.8 143.0 %all-gather.6.cloned.1.call-done = bf16[16,132,2560]{2,1,0:T(8,128)(2,1)} async-done(((bf16[1,132,2560]{2,1,0:T(8,128)(2,1)}), bf16[16,132,2560]{2,1,0:T(8,128)(2,1)}) %all-gather.6.cloned.1.call-update) | async-done | bytes 10813456 | tf_op jit(solution)/shard_map/all_gather | solution.py:168
  290.8 11.0 %reshape.163 = bf16[2112,2560]{1,0:T(8,128)(2,1)} reshape(bf16[16,132,2560]{2,1,0:T(8,128)(2,1)} %all-gather.6.cloned.1.call-done) | data formatting | bytes 21626880
  301.8 10.3 %fusion.63 = f32[2112,320]{1,0:T(8,128)} fusion(bf16[2112,2560]{1,0:T(8,128)(2,1)} %reshape.163, bf16[2560,320]{0,1:T(8,128)(2,1)S(1)} %copy-done), kind=kOutput, calls=%fused_computation.120 | convolution fusion | flops 3460300800 | bytes 15155200 | tf_op jit(solution)/shard_map/dot_general | solution.py:169
  312.0 4.2 reshape.129
  316.3 2.9 dynamic-slice_bitcast_fusion
  322.7 2.1 collective-permute-start.3
  325.0 3.8 collective-permute-done
  334.0 2.2 collective-permute-start.7
  342.4 4.1 collective-permute-done.5
  348.7 4.1 collective-permute-start.11
  353.5 15.2 %collective-permute-done.7 = f32[132,320]{1,0:T(8,128)S(1)} collective-permute-done((f32[132,320]{1,0:T(8,128)S(1)}, f32[132,320]{1,0:T(8,128)S(1)}, u32[]{:S(2)}, u32[]{:S(2)}) %collective-permute-start.7) | collective-permute-done | bytes 168992 | tf_op jit(solution)/shard_map/ppermute | solution.py:37
  369.4 3.8 collective-permute-done.8
  373.3 6.4 %collective-permute-start.13 = (f32[132,320]{1,0:T(8,128)S(1)}, f32[132,320]{1,0:T(8,128)S(1)}, u32[]{:S(2)}, u32[]{:S(2)}) collective-permute-start(f32[132,320]{1,0:T(8,128)S(1)} %get-tuple-element.55), channel_id=1, source_target_pairs={{0,28},{2,30},{4,24},{6,26},{8,20},{10,22},{12,16},{14,18},{16,12}... | collective-permute-start | bytes 506888 | tf_op jit(solution)/shard_map/ppermute | solution.py:37
  380.3 3.6 collective-permute-start.14
  384.7 4.2 collective-permute-done.10
  389.6 7.6 %collective-permute-done.11 = f32[132,320]{1,0:T(8,128)S(1)} collective-permute-done((f32[132,320]{1,0:T(8,128)S(1)}, f32[132,320]{1,0:T(8,128)S(1)}, u32[]{:S(2)}, u32[]{:S(2)}) %collective-permute-start.11) | collective-permute-done | bytes 168992 | tf_op jit(solution)/shard_map/ppermute | solution.py:37
  397.8 4.3 collective-permute-done.12
  402.9 3.0 collective-permute-done.13
  408.8 4.4 gather_fusion.1
  413.2 4.3 copy.67
  417.5 4.7 reshape.130
  422.3 12.5 %reduce-scatter.2.cloned.1.call-done = f32[132,2560]{1,0:T(8,128)} async-done(((f32[132,5120]{1,0:T(8,128)}), f32[132,2560]{1,0:T(8,128)}) %reduce-scatter.2.cloned.1.call-update) | async-done | bytes 1351696 | tf_op jit(solution)/shard_map/reduce_scatter | solution.py:171
  436.3 31.5 %all-gather.3 = bf16[32,1,2560]{2,1,0:T(2,128)(2,1)S(1)} all-gather(bf16[1,1,2560]{2,1,0:T(2,128)(2,1)S(1)} %slice_bitcast_fusion), channel_id=1, replica_groups=mesh['seq'=16,'tp'=2] {'seq','tp'}, dimensions={0}, use_global_device_ids=true | all-gather | bytes 168960 | tf_op jit(solution)/shard_map/all_gather | solution.py:176
  470.9 19.8 %fusion.61 = (f32[20]{0:T(128)S(1)}, f32[20,4752]{1,0:T(8,128)S(1)}) fusion(bf16[5120,4752]{0,1:T(8,128)(2,1)} %param.29, f32[5120]{0:T(1024)S(1)} %convert_element_type.43, f32[20]{0:T(128)S(1)} %add_rsqrt_fusion, bf16[16,5120]{1,0:T(8,128)(2,1)S(1)} %reshape.131, bf16[4,5120]{1,0:T(4,128)(2,1)S(1)} %all_gather.22), kind=kOutput, calls=%fused_computation.118 | convolution fusion | flops 974021440 | bytes 49266080 | tf_op jit(solution)/shard_map/dot_general | solution.py:187
  491.5 49.9 %all-reduce.2 = (f32[640]{0:T(1024)S(1)}, f32[640]{0:T(1024)S(1)}) all-reduce(f32[640]{0:T(1024)S(1)} %dynamic-update-slice, f32[640]{0:T(1024)S(1)} %dynamic-update-slice.1), channel_id=2, replica_groups=mesh['seq'=16,'tp'=2] {'seq','tp'}, use_global_device_ids=true, to_apply=%add | all-reduce | flops 1280 | bytes 10240
  (149 shorter events, 52.4 us)
Async XLA Ops:
  7.2 294.6 %copy-start = (bf16[2560,320]{0,1:T(8,128)(2,1)S(1)}, bf16[2560,320]{0,1:T(8,128)(2,1)}, u32[]{:S(2)}) copy-start(bf16[2560,320]{0,1:T(8,128)(2,1)} %param.27) | copy-start | bytes 4915204
  7.2 283.6 %all-gather.6.cloned.1.call-start = ((), (), s32[]{:S(2)}) async-start(), calls=%async_computation.2 | async-start | bytes 11837440 | tf_op jit(solution)/shard_map/all_gather | solution.py:168
  15.5 7.8 %copy-start.2 = (bf16[768,4,128]{2,0,1:T(8,128)(2,1)S(1)}, bf16[768,4,128]{2,0,1:T(8,128)(2,1)}, u32[]{:S(2)}) copy-start(bf16[768,4,128]{2,0,1:T(8,128)(2,1)} %copy.56) | copy-start | bytes 2359300
  23.3 7.4 %copy-start.3 = (bf16[1,1,768,512]{2,3,1,0:T(8,128)(2,1)S(1)}, bf16[1,1,768,512]{2,3,1,0:T(8,128)(2,1)}, u32[]{:S(2)}) copy-start(bf16[1,1,768,512]{2,3,1,0:T(8,128)(2,1)} %copy.52) | copy-start | bytes 2359300
  34.3 4.4 copy-start.7
  34.3 4.4 copy-start.10
  36.2 34.9 %copy-start.9 = (bf16[2,4,512]{2,1,0:T(4,128)(2,1)S(1)}, bf16[2,4,512]{2,1,0:T(4,128)(2,1)}, u32[]{:S(2)}) copy-start(bf16[2,4,512]{2,1,0:T(4,128)(2,1)} %param.23) | copy-start | bytes 24580
  147.5 287.3 %reduce-scatter.2.cloned.1.call-start = ((), (), s32[]{:S(2)}) async-start(), calls=%async_computation.1 | async-start | bytes 4177920 | tf_op jit(solution)/shard_map/reduce_scatter | solution.py:171
  319.2 9.6 %collective-permute-start = (f32[132,320]{1,0:T(8,128)S(1)}, f32[132,320]{1,0:T(8,128)S(1)}, u32[]{:S(2)}, u32[]{:S(2)}) collective-permute-start(f32[132,320]{1,0:T(8,128)S(1)} %get-tuple-element.68), channel_id=1, source_target_pairs={{0,2},{2,0},{4,6},{6,4},{8,10},{10,8},{12,14},{14,12},{16,18},{18,... | collective-permute-start | bytes 506888 | tf_op jit(solution)/shard_map/ppermute | solution.py:37
  319.9 11.5 %collective-permute-start.1 = (f32[132,320]{1,0:T(8,128)S(1)}, f32[132,320]{1,0:T(8,128)S(1)}, u32[]{:S(2)}, u32[]{:S(2)}) collective-permute-start(f32[132,320]{1,0:T(8,128)S(1)} %get-tuple-element.67), channel_id=1, source_target_pairs={{0,4},{2,6},{4,0},{6,2},{8,12},{10,14},{12,8},{14,10},{16,20},{18,... | collective-permute-start | bytes 506888 | tf_op jit(solution)/shard_map/ppermute | solution.py:37
  321.5 12.5 %collective-permute-start.2 = (f32[132,320]{1,0:T(8,128)S(1)}, f32[132,320]{1,0:T(8,128)S(1)}, u32[]{:S(2)}, u32[]{:S(2)}) collective-permute-start(f32[132,320]{1,0:T(8,128)S(1)} %get-tuple-element.66), channel_id=1, source_target_pairs={{0,6},{2,4},{4,2},{6,0},{8,14},{10,12},{12,10},{14,8},{16,22},{18,... | collective-permute-start | bytes 506888 | tf_op jit(solution)/shard_map/ppermute | solution.py:37
  322.7 14.2 %collective-permute-start.3 = (f32[132,320]{1,0:T(8,128)S(1)}, f32[132,320]{1,0:T(8,128)S(1)}, u32[]{:S(2)}, u32[]{:S(2)}) collective-permute-start(f32[132,320]{1,0:T(8,128)S(1)} %get-tuple-element.65), channel_id=1, source_target_pairs={{0,8},{2,10},{4,12},{6,14},{8,0},{10,2},{12,4},{14,6},{16,24},{18,... | collective-permute-start | bytes 506888 | tf_op jit(solution)/shard_map/ppermute | solution.py:37
  324.8 15.3 %collective-permute-start.4 = (f32[132,320]{1,0:T(8,128)S(1)}, f32[132,320]{1,0:T(8,128)S(1)}, u32[]{:S(2)}, u32[]{:S(2)}) collective-permute-start(f32[132,320]{1,0:T(8,128)S(1)} %get-tuple-element.64), channel_id=1, source_target_pairs={{0,10},{2,8},{4,14},{6,12},{8,2},{10,0},{12,6},{14,4},{16,26},{18,... | collective-permute-start | bytes 506888 | tf_op jit(solution)/shard_map/ppermute | solution.py:37
  328.8 17.7 %collective-permute-start.5 = (f32[132,320]{1,0:T(8,128)S(1)}, f32[132,320]{1,0:T(8,128)S(1)}, u32[]{:S(2)}, u32[]{:S(2)}) collective-permute-start(f32[132,320]{1,0:T(8,128)S(1)} %get-tuple-element.63), channel_id=1, source_target_pairs={{0,12},{2,14},{4,8},{6,10},{8,4},{10,6},{12,0},{14,2},{16,28},{18,... | collective-permute-start | bytes 506888 | tf_op jit(solution)/shard_map/ppermute | solution.py:37
  331.4 17.3 %collective-permute-start.6 = (f32[132,320]{1,0:T(8,128)S(1)}, f32[132,320]{1,0:T(8,128)S(1)}, u32[]{:S(2)}, u32[]{:S(2)}) collective-permute-start(f32[132,320]{1,0:T(8,128)S(1)} %get-tuple-element.62), channel_id=1, source_target_pairs={{0,14},{2,12},{4,10},{6,8},{8,6},{10,4},{12,2},{14,0},{16,30},{18,... | collective-permute-start | bytes 506888 | tf_op jit(solution)/shard_map/ppermute | solution.py:37
  334.0 34.7 %collective-permute-start.7 = (f32[132,320]{1,0:T(8,128)S(1)}, f32[132,320]{1,0:T(8,128)S(1)}, u32[]{:S(2)}, u32[]{:S(2)}) collective-permute-start(f32[132,320]{1,0:T(8,128)S(1)} %get-tuple-element.61), channel_id=1, source_target_pairs={{0,16},{2,18},{4,20},{6,22},{8,24},{10,26},{12,28},{14,30},{16,0},... | collective-permute-start | bytes 506888 | tf_op jit(solution)/shard_map/ppermute | solution.py:37
  336.9 36.3 %collective-permute-start.8 = (f32[132,320]{1,0:T(8,128)S(1)}, f32[132,320]{1,0:T(8,128)S(1)}, u32[]{:S(2)}, u32[]{:S(2)}) collective-permute-start(f32[132,320]{1,0:T(8,128)S(1)} %get-tuple-element.60), channel_id=1, source_target_pairs={{0,18},{2,16},{4,22},{6,20},{8,26},{10,24},{12,30},{14,28},{16,2},... | collective-permute-start | bytes 506888 | tf_op jit(solution)/shard_map/ppermute | solution.py:37
  340.1 40.3 %collective-permute-start.9 = (f32[132,320]{1,0:T(8,128)S(1)}, f32[132,320]{1,0:T(8,128)S(1)}, u32[]{:S(2)}, u32[]{:S(2)}) collective-permute-start(f32[132,320]{1,0:T(8,128)S(1)} %get-tuple-element.59), channel_id=1, source_target_pairs={{0,20},{2,22},{4,16},{6,18},{8,28},{10,30},{12,24},{14,26},{16,4},... | collective-permute-start | bytes 506888 | tf_op jit(solution)/shard_map/ppermute | solution.py:37
  346.5 42.4 %collective-permute-start.10 = (f32[132,320]{1,0:T(8,128)S(1)}, f32[132,320]{1,0:T(8,128)S(1)}, u32[]{:S(2)}, u32[]{:S(2)}) collective-permute-start(f32[132,320]{1,0:T(8,128)S(1)} %get-tuple-element.58), channel_id=1, source_target_pairs={{0,22},{2,20},{4,18},{6,16},{8,30},{10,28},{12,26},{14,24},{16,6},... | collective-permute-start | bytes 506888 | tf_op jit(solution)/shard_map/ppermute | solution.py:37
  348.7 48.4 %collective-permute-start.11 = (f32[132,320]{1,0:T(8,128)S(1)}, f32[132,320]{1,0:T(8,128)S(1)}, u32[]{:S(2)}, u32[]{:S(2)}) collective-permute-start(f32[132,320]{1,0:T(8,128)S(1)} %get-tuple-element.57), channel_id=1, source_target_pairs={{0,24},{2,26},{4,28},{6,30},{8,16},{10,18},{12,20},{14,22},{16,8},... | collective-permute-start | bytes 506888 | tf_op jit(solution)/shard_map/ppermute | solution.py:37
  368.7 33.5 %collective-permute-start.12 = (f32[132,320]{1,0:T(8,128)S(1)}, f32[132,320]{1,0:T(8,128)S(1)}, u32[]{:S(2)}, u32[]{:S(2)}) collective-permute-start(f32[132,320]{1,0:T(8,128)S(1)} %get-tuple-element.56), channel_id=1, source_target_pairs={{0,26},{2,24},{4,30},{6,28},{8,18},{10,16},{12,22},{14,20},{16,10}... | collective-permute-start | bytes 506888 | tf_op jit(solution)/shard_map/ppermute | solution.py:37
  373.3 32.6 %collective-permute-start.13 = (f32[132,320]{1,0:T(8,128)S(1)}, f32[132,320]{1,0:T(8,128)S(1)}, u32[]{:S(2)}, u32[]{:S(2)}) collective-permute-start(f32[132,320]{1,0:T(8,128)S(1)} %get-tuple-element.55), channel_id=1, source_target_pairs={{0,28},{2,30},{4,24},{6,26},{8,20},{10,22},{12,16},{14,18},{16,12}... | collective-permute-start | bytes 506888 | tf_op jit(solution)/shard_map/ppermute | solution.py:37
  380.3 27.8 %collective-permute-start.14 = (f32[132,320]{1,0:T(8,128)S(1)}, f32[132,320]{1,0:T(8,128)S(1)}, u32[]{:S(2)}, u32[]{:S(2)}) collective-permute-start(f32[132,320]{1,0:T(8,128)S(1)} %get-tuple-element.54), channel_id=1, source_target_pairs={{0,30},{2,28},{4,26},{6,24},{8,22},{10,20},{12,18},{14,16},{16,14}... | collective-permute-start | bytes 506888 | tf_op jit(solution)/shard_map/ppermute | solution.py:37
  417.5 4.8 copy-start.8
  417.5 17.3 %copy-start.4 = (bf16[128,2560]{1,0:T(8,128)(2,1)S(1)}, bf16[128,2560]{1,0:T(8,128)(2,1)}, u32[]{:S(2)}) copy-start(bf16[128,2560]{1,0:T(8,128)(2,1)} %param.16) | copy-start | bytes 1966084
  417.5 17.3 %copy-start.6 = (bf16[4,2560]{1,0:T(4,128)(2,1)S(1)}, bf16[4,2560]{1,0:T(4,128)(2,1)}, u32[]{:S(2)}) copy-start(bf16[4,2560]{1,0:T(4,128)(2,1)} %param.21) | copy-start | bytes 61444
  436.3 54.4 %copy-start.5 = (bf16[4,2560]{1,0:T(4,128)(2,1)}, bf16[4,2560]{1,0:T(4,128)(2,1)S(1)}, u32[]{:S(2)}) copy-start(bf16[4,2560]{1,0:T(4,128)(2,1)S(1)} %slice.72) | copy-start | bytes 61444
  470.9 73.9 %copy-start.1 = (bf16[2560,320]{0,1:T(8,128)(2,1)S(1)}, bf16[2560,320]{0,1:T(8,128)(2,1)}, u32[]{:S(2)}) copy-start(bf16[2560,320]{0,1:T(8,128)(2,1)} %param.27) | copy-start | bytes 4915204
Sparse Core Ops, SparseCore 0:
  147.6 143.1 all-gather.5
  422.4 12.3 reduce-scatter.1
